TPU v7x, 512 devices: a whole 4x8x8 slice. The times are simulated.
512 devices in a mesh: req: 64 (over x, z, core), tp: 8 (over y).
Axes of the slice: x: 4, y: 8, z: 8, core: 2. Of those that a mesh axis runs over, the one named last changes fastest.
Arguments:
- residual_input: bfloat16 [8192, 3584], P('req', 'tp'), may hold values from -6 to 6
- new_token_queries: bfloat16 [8192, 4096], P('req', 'tp'), may hold values from -8 to 8
- new_token_keys: bfloat16 [8192, 2048], P('req', 'tp'), may hold values from -8 to 8
- new_token_values: bfloat16 [8192, 2048], P('req', 'tp'), may hold values from -6 to 6
- key_page_pool: bfloat16 [1536, 16, 2048], P('req', None, 'tp'), may hold values from -6 to 6
- value_page_pool: bfloat16 [1536, 16, 2048], P('req', None, 'tp'), may hold values from -6 to 6
- request_page_table: int32 [128, 64], P('req'), may hold values from -1 to 23, as said below
- page_token_length: int32 [128, 64], P('req'), may hold values from 0 to 16, as said below
- request_token_length: int32 [64, 2], P('req'), may hold values from 1 to 96, 128 in all within a row
- request_adapter: int32 [64, 2], P('req'), may hold values from 0 to 63
- adapter_table_row: int32 [64], replicated, may hold values from 0 to 63, each once
- output_weight: bfloat16 [4096, 3584], P('tp'), may hold values from -0.125 to 0.125
- adapter_down_weight: bfloat16 [64, 16, 4096], P('req', None, 'tp'), may hold values from -0.09375 to 0.09375
- adapter_up_weight: bfloat16 [64, 16, 3584], P('req', None, 'tp'), may hold values from -1.5 to 1.5
- norm_scale_row: float32 [3584], P('tp'), may hold values from 0.25 to 1.75
Outputs:
- hidden_out: bfloat16 [8192, 3584], P('req', 'tp')
Inputs may be any that keep to these rules, and one draw needn't show every extreme that they name: request_page_table[q, o] is a page of the pool of owner o (rows o * 24 to o * 24 + 23 of the pools), or -1; so the 2 requests of one index of req take at most 2 pages from one owner, and in every draw the requests of some index of req each take a page from every owner. Requests may share pages. `page_token_length`: 0 exactly where request_page_table is -1; every used page of a request is full but at most one.
All inputs are finite; a program needn't handle non-finite values.
Results may differ from a plain program's by a relative error of at most 0.015.
Values may be sent and summed in bfloat16 or wider, within the bound.
No kernel may reach another device: no remote copies, remote signals or barrier semaphores. Data moves between devices by JAX's collectives and lax.ppermute only.
A program may use at most 64 MiB of HBM per device.

v0:
```python
import jax
import jax.numpy as jnp
from jax import lax
from jax.sharding import PartitionSpec as P

HEAD_SIZE = 256
epsilon = 1e-06
adapter_scale = 2.0
masked_score = -1e30


def attend(query_rows, new_keys, new_values, gathered_keys, gathered_values, usable, owner_request):
    token_count = query_rows.shape[0]
    kv_heads = new_keys.shape[1] // HEAD_SIZE
    group_size = query_rows.shape[1] // new_keys.shape[1]
    requests_here = gathered_keys.shape[0]
    cached_count = gathered_keys.shape[1]
    query_heads = query_rows.reshape(token_count, kv_heads, group_size, HEAD_SIZE)
    past_keys = gathered_keys.reshape(requests_here, cached_count, kv_heads, HEAD_SIZE)
    past_values = gathered_values.reshape(requests_here * cached_count, kv_heads, HEAD_SIZE)
    fresh_keys = new_keys.reshape(token_count, kv_heads, HEAD_SIZE)
    fresh_values = new_values.reshape(token_count, kv_heads, HEAD_SIZE)
    positions = jnp.arange(token_count, dtype=jnp.int32)
    scaling = HEAD_SIZE ** (-0.5)
    past_scores = (
        jnp.einsum("tgqd,rngd->tgqrn", query_heads, past_keys, preferred_element_type=jnp.float32)
        * scaling
    )
    past_mask = usable[None, :, :] & (
        owner_request[:, None, None] == jnp.arange(requests_here, dtype=jnp.int32)[None, :, None]
    )
    past_scores = jnp.where(past_mask[:, None, None, :, :], past_scores, masked_score)
    past_scores = past_scores.reshape(
        token_count, kv_heads, group_size, requests_here * cached_count
    )
    fresh_scores = (
        jnp.einsum("tgqd,ugd->tgqu", query_heads, fresh_keys, preferred_element_type=jnp.float32)
        * scaling
    )
    fresh_mask = (owner_request[:, None] == owner_request[None, :]) & (
        positions[None, :] <= positions[:, None]
    )
    fresh_scores = jnp.where(fresh_mask[:, None, None, :], fresh_scores, masked_score)
    scores = jnp.concatenate([past_scores, fresh_scores], axis=3)
    highest = jnp.max(scores, axis=3, keepdims=True)
    weights = jnp.exp(scores - highest)
    weights = (weights / jnp.sum(weights, axis=3, keepdims=True)).astype(jnp.bfloat16)
    all_values = jnp.concatenate([past_values, fresh_values], axis=0)
    mixed = jnp.einsum("tgqk,kgd->tgqd", weights, all_values, preferred_element_type=jnp.float32)
    return mixed.reshape(token_count, -1).astype(jnp.bfloat16)


def local(
    residual_input,
    new_token_queries,
    new_token_keys,
    new_token_values,
    key_page_pool,
    value_page_pool,
    request_page_table,
    page_token_length,
    request_token_length,
    request_adapter,
    adapter_table_row,
    output_weight,
    adapter_down_weight,
    adapter_up_weight,
    norm_scale_row,
):
    owners = lax.axis_size("req")
    groups = lax.axis_size("tp")
    requests_here = request_page_table.shape[0]
    page_rows = key_page_pool.shape[1]
    token_count = new_token_queries.shape[0]
    width_part = residual_input.shape[1]
    head_cols = key_page_pool.shape[2]
    down_cols = adapter_down_weight.shape[2]
    adapter_pair = jnp.concatenate([adapter_down_weight, adapter_up_weight], axis=2)
    adapters_everywhere = lax.all_gather(adapter_pair, "req", axis=0, tiled=True)
    wanted = lax.all_to_all(request_page_table, "req", split_axis=1, concat_axis=1, tiled=True)
    page_picks = jnp.maximum(wanted, 0)
    kv_pool = jnp.concatenate([key_page_pool, value_page_pool], axis=2)
    kv_out = kv_pool[page_picks]
    kv_back = lax.all_to_all(kv_out, "req", split_axis=1, concat_axis=1, tiled=True)
    kv_back = kv_back.reshape(requests_here, owners * page_rows, 2 * head_cols)
    gathered_keys = kv_back[:, :, :head_cols]
    gathered_values = kv_back[:, :, head_cols:]
    usable = (
        jnp.arange(page_rows, dtype=jnp.int32)[None, None, :] < page_token_length[:, :, None]
    ).reshape(requests_here, owners * page_rows)
    lengths = request_token_length[0]
    positions = jnp.arange(token_count, dtype=jnp.int32)
    ends = jnp.cumsum(lengths)
    owner_request = jnp.sum((positions[:, None] >= ends[None, :]).astype(jnp.int32), axis=1)
    attention = attend(
        new_token_queries,
        new_token_keys,
        new_token_values,
        gathered_keys,
        gathered_values,
        usable,
        owner_request,
    )
    adapters_all = adapter_table_row.shape[0]
    matches = request_adapter[0][:, None] == jnp.arange(adapters_all, dtype=jnp.int32)[None, :]
    chosen_pages = jnp.sum(jnp.where(matches, adapter_table_row[None, :], 0), axis=1)
    rows_here = adapters_everywhere.shape[0]
    picker = (chosen_pages[:, None] == jnp.arange(rows_here, dtype=jnp.int32)[None, :]).astype(
        jnp.bfloat16
    )
    selected = jnp.einsum(
        "rk,kab->rab", picker, adapters_everywhere, preferred_element_type=jnp.float32
    ).astype(jnp.bfloat16)
    adapter_in = selected[:, :, :down_cols]
    adapter_out = selected[:, :, down_cols:]
    rank_size = adapter_in.shape[1]
    selector = (
        owner_request[:, None] == jnp.arange(requests_here, dtype=jnp.int32)[None, :]
    ).astype(jnp.float32)
    selector_half = selector.astype(jnp.bfloat16)
    base_part = jnp.dot(attention, output_weight, preferred_element_type=jnp.float32)
    low_terms = jnp.einsum("tc,rkc->trk", attention, adapter_in, preferred_element_type=jnp.float32)
    low_part = jnp.sum(low_terms * selector[:, :, None], axis=1)
    base_slots = base_part.astype(jnp.bfloat16).reshape(token_count, groups, width_part)
    base_slots = jnp.transpose(base_slots, (1, 0, 2))
    low_slots = jnp.broadcast_to(
        low_part.astype(jnp.bfloat16)[None], (groups, token_count, rank_size)
    )
    pad_cols = -(width_part + rank_size) % 128
    slots = jnp.concatenate(
        [base_slots, low_slots, jnp.zeros((groups, token_count, pad_cols), jnp.bfloat16)], axis=2
    )
    arrived = lax.all_to_all(slots, "tp", split_axis=0, concat_axis=0, tiled=True)
    arrived = arrived.astype(jnp.float32)
    base_local = jnp.sum(arrived[:, :, :width_part], axis=0)
    low_sum = jnp.sum(arrived[:, :, width_part : width_part + rank_size], axis=0)
    rows_masked = (low_sum.astype(jnp.bfloat16)[:, None, :] * selector_half[:, :, None]).reshape(
        token_count, requests_here * rank_size
    )
    projected = base_local + adapter_scale * jnp.dot(
        rows_masked,
        adapter_out.reshape(requests_here * rank_size, width_part),
        preferred_element_type=jnp.float32,
    )
    square_part = jnp.sum(projected * projected, axis=1)
    square_sum = lax.psum(square_part, "tp")
    mean_square = square_sum / (groups * width_part)
    scaled = projected * lax.rsqrt(mean_square + epsilon)[:, None]
    return (residual_input.astype(jnp.float32) + scaled * norm_scale_row).astype(jnp.bfloat16)


def solution(mesh):
    in_specs = (
        P("req", "tp"),
        P("req", "tp"),
        P("req", "tp"),
        P("req", "tp"),
        P("req", None, "tp"),
        P("req", None, "tp"),
        P("req", None),
        P("req", None),
        P("req", None),
        P("req", None),
        P(),
        P("tp", None),
        P("req", None, "tp"),
        P("req", None, "tp"),
        P("tp"),
    )
    out_specs = P("req", "tp")
    return jax.shard_map(local, mesh=mesh, in_specs=in_specs, out_specs=out_specs, check_vma=False)
```

profile of v0, /device:TPU:8, one launch (start us, length us, event | category | flops | bytes accessed | tf_op | source)
XLA Modules:
  0.0 186.8 jit_solution(3870955451242989684)
XLA Ops:
  6.5 1.4 copy.88
  8.0 13.8 %all-to-all-start = ((s32[2,64,1]{0,2,1:T(1,128)}), s32[2,64,1]{0,2,1:T(1,128)S(1)}, u32[]{:S(2)}, u32[]{:S(2)}) async-start(s32[2,64,1]{0,2,1:T(1,128)} %copy.88), calls=%async_computation | async-start | bytes 65536 | tf_op jit(solution)/shard_map/all_to_all | solution.py:80
  21.8 1.4 pad_maximum_fusion.1
  23.2 1.1 pad_maximum_fusion
  24.2 7.0 %all-to-all-done = s32[2,64,1]{0,2,1:T(1,128)S(1)} async-done(((s32[2,64,1]{0,2,1:T(1,128)}), s32[2,64,1]{0,2,1:T(1,128)S(1)}, u32[]{:S(2)}, u32[]{:S(2)}) %all-to-all-start) | async-done | bytes 544 | tf_op jit(solution)/shard_map/all_to_all | solution.py:80
  31.4 0.7 gather_fusion
  32.1 1.6 copy.90
  33.7 4.8 %all-to-all-start.1 = ((bf16[2,64,16,512]{3,2,0,1:T(8,128)(2,1)}), bf16[2,64,16,512]{3,2,0,1:T(8,128)(2,1)S(1)}, u32[]{:S(2)}, u32[]{:S(2)}) async-start(bf16[2,64,16,512]{3,2,0,1:T(8,128)(2,1)} %copy.90), calls=%async_computation.1 | async-start | bytes 4194304 | tf_op jit(solution)/shard_map/all_to_all | solution.py:84
  38.5 0.7 copy.92
  40.6 0.9 fusion.38
  41.4 71.5 %all-gather.2.cloned.1.call-done = bf16[64,16,960]{2,1,0:T(8,128)(2,1)} async-done(((bf16[1,16,960]{2,1,0:T(8,128)(2,1)}), bf16[64,16,960]{2,1,0:T(8,128)(2,1)}) %all-gather.2.cloned.1.call-update) | async-done | bytes 1966096 | tf_op jit(solution)/shard_map/all_gather | solution.py:79
  112.9 3.9 %fusion.10 = bf16[2,16,960]{2,0,1:T(2,128)(2,1)S(1)} fusion(bf16[64,16,960]{2,1,0:T(8,128)(2,1)} %all-gather.2.cloned.1.call-done, s32[2]{0:T(128)S(1)} %fusion.31), kind=kOutput, calls=%fused_computation.19 | convolution fusion | flops 3963008 | bytes 2027528 | tf_op jit(solution)/shard_map/rk,kab->rab/dot_general | solution.py:111
  117.4 1.3 copy-done.1
  118.9 1.4 copy.93
  120.8 1.4 fusion.37
  122.5 0.7 copy-done.6
  124.2 1.5 copy-done.3
  125.7 0.7 convolution_convert_fusion
  126.4 0.6 copy.99
  127.2 1.3 maximum_maximum_fusion
  128.4 6.8 %all-to-all-start.2 = ((bf16[8,128,512]{1,2,0:T(8,128)(2,1)}), bf16[8,128,512]{1,2,0:T(8,128)(2,1)S(1)}, u32[]{:S(2)}, u32[]{:S(2)}) async-start(bf16[8,128,512]{1,2,0:T(8,128)(2,1)} %maximum_maximum_fusion), calls=%async_computation.2 | async-start | bytes 2097152 | tf_op jit(solution)/shard_map/all_to_all | solution.py:133
  135.3 27.7 %all-to-all-done.2 = bf16[8,128,512]{1,2,0:T(8,128)(2,1)S(1)} async-done(((bf16[8,128,512]{1,2,0:T(8,128)(2,1)}), bf16[8,128,512]{1,2,0:T(8,128)(2,1)S(1)}, u32[]{:S(2)}, u32[]{:S(2)}) %all-to-all-start.2) | async-done | bytes 1048608 | tf_op jit(solution)/shard_map/all_to_all | solution.py:133
  163.5 15.6 %psum.7 = f32[128]{0:T(128)S(1)} all-reduce(f32[128]{0:T(128)S(1)} %get-tuple-element.12), channel_id=1, replica_groups=mesh['req'=64,'tp'=8] {'tp'}, use_global_device_ids=true, to_apply=%region_10.11 | all-reduce | flops 128 | bytes 1024 | tf_op jit(solution)/shard_map/psum | solution.py:146
  179.1 0.8 add_convert_fusion
  (66 shorter events, 4.6 us)
Async XLA Ops:
  6.5 34.0 %copy-start = (bf16[128,256]{1,0:T(8,128)(2,1)S(1)}, bf16[128,256]{1,0:T(8,128)(2,1)}, u32[]{:S(2)}) copy-start(bf16[128,256]{1,0:T(8,128)(2,1)} %param.17) | copy-start | bytes 196612
  8.0 23.2 %all-to-all-start = ((s32[2,64,1]{0,2,1:T(1,128)}), s32[2,64,1]{0,2,1:T(1,128)S(1)}, u32[]{:S(2)}, u32[]{:S(2)}) async-start(s32[2,64,1]{0,2,1:T(1,128)} %copy.88), calls=%async_computation | async-start | bytes 65536 | tf_op jit(solution)/shard_map/all_to_all | solution.py:80
  21.7 91.2 %all-gather.2.cloned.1.call-start = ((), (), s32[]{:S(2)}) async-start(), calls=%async_computation.3 | async-start | bytes 2129920 | tf_op jit(solution)/shard_map/all_gather | solution.py:79
  33.7 4.9 %copy-start.8 = (bf16[128,256]{1,0:T(8,128)(2,1)S(1)}, bf16[128,256]{1,0:T(8,128)(2,1)}, u32[]{:S(2)}) copy-start(bf16[128,256]{1,0:T(8,128)(2,1)} %param.18) | copy-start | bytes 196612
  33.7 5.6 %copy-start.11 = (s32[2,64]{1,0:T(2,128)S(1)}, s32[2,64]{1,0:T(2,128)}, u32[]{:S(2)}) copy-start(s32[2,64]{1,0:T(2,128)} %param.22) | copy-start | bytes 1540
  33.7 5.9 %copy-start.13 = (s32[1,2]{1,0:T(1,128)S(1)}, s32[1,2]{1,0:T(1,128)}, u32[]{:S(2)}) copy-start(s32[1,2]{1,0:T(1,128)} %param.23) | copy-start | bytes 28
  33.7 6.2 %copy-start.14 = (s32[64]{0:T(128)S(1)}, s32[64]{0:T(128)}, u32[]{:S(2)}) copy-start(s32[64]{0:T(128)} %param.25) | copy-start | bytes 772
  33.7 6.2 %copy-start.15 = (s32[1,2]{1,0:T(1,128)S(1)}, s32[1,2]{1,0:T(1,128)}, u32[]{:S(2)}) copy-start(s32[1,2]{1,0:T(1,128)} %param.24) | copy-start | bytes 28
  33.7 6.9 %copy-start.12 = (bf16[128,512]{1,0:T(8,128)(2,1)S(1)}, bf16[128,512]{1,0:T(8,128)(2,1)}, u32[]{:S(2)}) copy-start(bf16[128,512]{1,0:T(8,128)(2,1)} %param.16) | copy-start | bytes 393220
  33.7 83.1 %all-to-all-start.1 = ((bf16[2,64,16,512]{3,2,0,1:T(8,128)(2,1)}), bf16[2,64,16,512]{3,2,0,1:T(8,128)(2,1)S(1)}, u32[]{:S(2)}, u32[]{:S(2)}) async-start(bf16[2,64,16,512]{3,2,0,1:T(8,128)(2,1)} %copy.90), calls=%async_computation.1 | async-start | bytes 4194304 | tf_op jit(solution)/shard_map/all_to_all | solution.py:84
  116.8 0.6 copy-start.5
  117.4 1.3 copy-start.1
  118.8 2.0 %copy-start.2 = (bf16[2,64,16,512]{3,2,1,0:T(8,128)(2,1)S(1)}, bf16[2,64,16,512]{3,2,1,0:T(8,128)(2,1)}, u32[]{:S(2)}) copy-start(bf16[2,64,16,512]{3,2,1,0:T(8,128)(2,1)} %copy-done.1) | copy-start | bytes 6291460
  122.3 0.9 copy-start.6
  122.4 1.2 copy-start.4
  122.4 1.2 copy-start.9
  123.7 2.0 %copy-start.3 = (bf16[512,3584]{1,0:T(8,128)(2,1)S(1)}, bf16[512,3584]{1,0:T(8,128)(2,1)}, u32[]{:S(2)}) copy-start(bf16[512,3584]{1,0:T(8,128)(2,1)} %param.26) | copy-start | bytes 11010052
  125.7 1.3 slice-start
  128.4 34.5 %all-to-all-start.2 = ((bf16[8,128,512]{1,2,0:T(8,128)(2,1)}), bf16[8,128,512]{1,2,0:T(8,128)(2,1)S(1)}, u32[]{:S(2)}, u32[]{:S(2)}) async-start(bf16[8,128,512]{1,2,0:T(8,128)(2,1)} %maximum_maximum_fusion), calls=%async_computation.2 | async-start | bytes 2097152 | tf_op jit(solution)/shard_map/all_to_all | solution.py:133
  135.3 27.9 %slice-start.1 = ((bf16[2,16,960]{2,0,1:T(2,128)(2,1)}), bf16[2,16,448]{2,0,1:T(2,128)(2,1)S(1)}, s32[]{:S(2)}) async-start(bf16[2,16,960]{2,0,1:T(2,128)(2,1)} %copy-done.5), calls=%async_computation.5 | async-start | bytes 65536 | tf_op jit(solution)/shard_map/slice | solution.py:115
  163.1 16.1 %copy-start.7 = (bf16[128,448]{0,1:T(8,128)(2,1)S(1)}, bf16[128,448]{0,1:T(8,128)(2,1)}, u32[]{:S(2)}) copy-start(bf16[128,448]{0,1:T(8,128)(2,1)} %param.15) | copy-start | bytes 344068
  163.1 16.1 %copy-start.10 = (f32[448]{0:T(512)S(1)}, f32[448]{0:T(512)}, u32[]{:S(2)}) copy-start(f32[448]{0:T(512)} %param.29) | copy-start | bytes 5380
Sparse Core Ops, SparseCore 0:
  25.9 86.9 all-gather.1
where the time goes:
time: 187 us
  waiting for transfers between devices  106 us (57%)
  starting transfers between devices  25.5 us (14%)
  blocking collectives  15.6 us (8%)
  between operations  13.7 us (7%)
  local copies, waits for them, and re-layouts  12.1 us (6%)
  matrix products  7.86 us (4%)
  other arithmetic  5.9 us (3%)
    all_gather x1, waiting for transfers between devices, local(): lax.all_gather(adapter_pair, 'req', axis=0, tiled=True)  71.5 us
    all_to_all x1, waiting for transfers between devices, local(): lax.all_to_all(slots, 'tp', split_axis=0, concat_axis=0, tiled=True)  27.7 us
    psum x1, blocking collectives, local(): square_sum = lax.psum(square_part, 'tp')  15.6 us
    all_to_all x1, starting transfers between devices, local(): lax.all_to_all(request_page_table, 'req', split_axis=1, concat_axis=1, ti...  13.8 us
    all_to_all x1, waiting for transfers between devices, local(): lax.all_to_all(request_page_table, 'req', split_axis=1, concat_axis=1, ti...  6.97 us
    all_to_all x1, starting transfers between devices, local(): lax.all_to_all(slots, 'tp', split_axis=0, concat_axis=0, tiled=True)  6.83 us
    unnamed x33, local copies, waits for them, and re-layouts  5.44 us
    all_to_all x1, starting transfers between devices, local(): lax.all_to_all(kv_out, 'req', split_axis=1, concat_axis=1, tiled=True)  4.84 us
  transfers between devices with their start and end apart: 4, of which 3 were waited for; matrix products, arithmetic and copies ran while one was open for 6% of the time, Pallas kernels for 0%

commit v1 on v0

--- a/solution.py
+++ b/solution.py
@@ -76,7 +76,9 @@
     head_cols = key_page_pool.shape[2]
     down_cols = adapter_down_weight.shape[2]
     adapter_pair = jnp.concatenate([adapter_down_weight, adapter_up_weight], axis=2)
-    adapters_everywhere = lax.all_gather(adapter_pair, "req", axis=0, tiled=True)
+    adapters_everywhere = jnp.concatenate(
+        lax.all_to_all(jnp.stack([adapter_pair] * lax.axis_size("req")), "req", 0, 0), axis=0
+    )
     wanted = lax.all_to_all(request_page_table, "req", split_axis=1, concat_axis=1, tiled=True)
     page_picks = jnp.maximum(wanted, 0)
     kv_pool = jnp.concatenate([key_page_pool, value_page_pool], axis=2)

time: 187 us -> 204 us (1.091)
  waiting for transfers between devices: 106 us -> 129 us
  between operations: 13.7 us -> 0.32 us
  starting transfers between devices: 25.5 us -> 32.9 us
    all_gather x1 -> x0, waiting for transfers between devices: 71.5 us -> none  [local(): lax.all_gather(adapter_pair, 'req', axis=0, tiled=True)]
    all_to_all x0 -> x1, waiting for transfers between devices: none -> 48.4 us  [local(): lax.all_to_all(jnp.stack([adapter_pair] * lax.axis_size('req')), 'req', 0...]
    all_to_all x1, waiting for transfers between devices: 0.01 us -> 44.4 us  [local(): lax.all_to_all(kv_out, 'req', split_axis=1, concat_axis=1, tiled=True)]
    all_to_all x0 -> x1, starting transfers between devices: none -> 5.7 us  [local(): lax.all_to_all(jnp.stack([adapter_pair] * lax.axis_size('req')), 'req', 0...]
    unnamed x33 -> x37, local copies, waits for them, and re-layouts: 5.44 us -> 5.01 us
  transfers between devices with their start and end apart: 4 -> 4, of which waited for: 3 -> 4; matrix products, arithmetic and copies ran while one was open for 6% -> 5% of each run, Pallas kernels for 0% -> 0%
where the time goes in v1:
time: 204 us; the launch traced here: 203 us
  waiting for transfers between devices  129 us (63%)
  starting transfers between devices  32.9 us (16%)
  blocking collectives  15.6 us (8%)
  local copies, waits for them, and re-layouts  13.2 us (6%)
  matrix products  7.84 us (4%)
  other arithmetic  4.26 us (2%)
    all_to_all x1, waiting for transfers between devices, local(): lax.all_to_all(jnp.stack([adapter_pair] * lax.axis_size('req')), 'req', 0...  48.4 us
    all_to_all x1, waiting for transfers between devices, local(): lax.all_to_all(kv_out, 'req', split_axis=1, concat_axis=1, tiled=True)  44.4 us
    all_to_all x1, waiting for transfers between devices, local(): lax.all_to_all(slots, 'tp', split_axis=0, concat_axis=0, tiled=True)  27.5 us
    psum x1, blocking collectives, local(): square_sum = lax.psum(square_part, 'tp')  15.6 us
    all_to_all x1, starting transfers between devices, local(): lax.all_to_all(request_page_table, 'req', split_axis=1, concat_axis=1, ti...  13.8 us
    all_to_all x1, waiting for transfers between devices, local(): lax.all_to_all(request_page_table, 'req', split_axis=1, concat_axis=1, ti...  8.71 us
    all_to_all x1, starting transfers between devices, local(): lax.all_to_all(slots, 'tp', split_axis=0, concat_axis=0, tiled=True)  7.56 us
    all_to_all x1, starting transfers between devices, local(): lax.all_to_all(kv_out, 'req', split_axis=1, concat_axis=1, tiled=True)  5.89 us
  transfers between devices with their start and end apart: 4, of which 4 were waited for; matrix products, arithmetic and copies ran while one was open for 5% of the time, Pallas kernels for 0%

profile of v1, /device:TPU:8, one launch (start us, length us, event | category | flops | bytes accessed | tf_op | source)
XLA Modules:
  0.0 203.3 jit_solution(11416308881236625925)
XLA Ops:
  0.0 1.4 copy.84
  1.4 13.8 %all-to-all-start = ((s32[2,64,1]{0,2,1:T(1,128)}), s32[2,64,1]{0,2,1:T(1,128)S(1)}, u32[]{:S(2)}, u32[]{:S(2)}) async-start(s32[2,64,1]{0,2,1:T(1,128)} %copy.84), calls=%async_computation | async-start | bytes 65536 | tf_op jit(solution)/shard_map/all_to_all | solution.py:82
  15.2 0.7 maximum_bitcast_fusion.2
  16.0 8.7 %all-to-all-done = s32[2,64,1]{0,2,1:T(1,128)S(1)} async-done(((s32[2,64,1]{0,2,1:T(1,128)}), s32[2,64,1]{0,2,1:T(1,128)S(1)}, u32[]{:S(2)}, u32[]{:S(2)}) %all-to-all-start) | async-done | bytes 544 | tf_op jit(solution)/shard_map/all_to_all | solution.py:82
  24.7 1.6 stack.2
  26.2 5.7 %all-to-all-start.2 = ((bf16[64,1,16,960]{3,2,1,0:T(8,128)(2,1)}), bf16[64,1,16,960]{3,2,1,0:T(8,128)(2,1)}, u32[]{:S(2)}, u32[]{:S(2)}) async-start(bf16[64,1,16,960]{3,2,1,0:T(8,128)(2,1)} %stack.2), calls=%async_computation.2 | async-start | bytes 4194304 | tf_op jit(solution)/shard_map/all_to_all | solution.py:80
  32.2 0.7 gather_fusion
  32.9 1.6 copy.86
  34.5 48.4 %all-to-all-done.2 = bf16[64,1,16,960]{3,2,1,0:T(8,128)(2,1)} async-done(((bf16[64,1,16,960]{3,2,1,0:T(8,128)(2,1)}), bf16[64,1,16,960]{3,2,1,0:T(8,128)(2,1)}, u32[]{:S(2)}, u32[]{:S(2)}) %all-to-all-start.2) | async-done | bytes 1966112 | tf_op jit(solution)/shard_map/all_to_all | solution.py:80
  82.9 5.9 %all-to-all-start.1 = ((bf16[2,64,16,512]{3,2,0,1:T(8,128)(2,1)}), bf16[2,64,16,512]{3,2,0,1:T(8,128)(2,1)S(1)}, u32[]{:S(2)}, u32[]{:S(2)}) async-start(bf16[2,64,16,512]{3,2,0,1:T(8,128)(2,1)} %copy.86), calls=%async_computation.1 | async-start | bytes 4194304 | tf_op jit(solution)/shard_map/all_to_all | solution.py:86
  88.8 0.7 copy.88
  90.9 0.8 fusion.39
  91.7 3.9 %fusion.11 = bf16[2,16,960]{2,0,1:T(2,128)(2,1)S(1)} fusion(bf16[64,1,16,960]{3,2,1,0:T(8,128)(2,1)} %all-to-all-done.2, s32[2]{0:T(128)S(1)} %fusion.32), kind=kOutput, calls=%fused_computation.20 | convolution fusion | flops 3963008 | bytes 2027528 | tf_op jit(solution)/shard_map/rk,kab->rab/dot_general | solution.py:113
  95.6 44.4 %all-to-all-done.1 = bf16[2,64,16,512]{3,2,0,1:T(8,128)(2,1)S(1)} async-done(((bf16[2,64,16,512]{3,2,0,1:T(8,128)(2,1)}), bf16[2,64,16,512]{3,2,0,1:T(8,128)(2,1)S(1)}, u32[]{:S(2)}, u32[]{:S(2)}) %all-to-all-start.1) | async-done | bytes 2097184 | tf_op jit(solution)/shard_map/all_to_all | solution.py:86
  140.2 1.3 copy-done.1
  141.6 1.4 copy.89
  143.6 1.4 fusion.38
  145.2 0.7 copy-done.8
  147.0 1.5 copy-done.3
  149.9 1.3 maximum_maximum_fusion
  151.2 7.6 %all-to-all-start.3 = ((bf16[8,128,512]{1,2,0:T(8,128)(2,1)}), bf16[8,128,512]{1,2,0:T(8,128)(2,1)S(1)}, u32[]{:S(2)}, u32[]{:S(2)}) async-start(bf16[8,128,512]{1,2,0:T(8,128)(2,1)} %maximum_maximum_fusion), calls=%async_computation.3 | async-start | bytes 2097152 | tf_op jit(solution)/shard_map/all_to_all | solution.py:135
  158.7 27.5 %all-to-all-done.3 = bf16[8,128,512]{1,2,0:T(8,128)(2,1)S(1)} async-done(((bf16[8,128,512]{1,2,0:T(8,128)(2,1)}), bf16[8,128,512]{1,2,0:T(8,128)(2,1)S(1)}, u32[]{:S(2)}, u32[]{:S(2)}) %all-to-all-start.3) | async-done | bytes 1048608 | tf_op jit(solution)/shard_map/all_to_all | solution.py:135
  186.8 15.6 %psum.7 = f32[128]{0:T(128)S(1)} all-reduce(f32[128]{0:T(128)S(1)} %get-tuple-element.12), channel_id=1, replica_groups=mesh['req'=64,'tp'=8] {'tp'}, use_global_device_ids=true, to_apply=%region_10.11 | all-reduce | flops 128 | bytes 1024 | tf_op jit(solution)/shard_map/psum | solution.py:148
  202.5 0.8 add_convert_fusion
  (70 shorter events, 5.4 us)
Async XLA Ops:
  0.0 90.9 %copy-start = (bf16[128,256]{1,0:T(8,128)(2,1)S(1)}, bf16[128,256]{1,0:T(8,128)(2,1)}, u32[]{:S(2)}) copy-start(bf16[128,256]{1,0:T(8,128)(2,1)} %param.17) | copy-start | bytes 196612
  1.4 23.2 %all-to-all-start = ((s32[2,64,1]{0,2,1:T(1,128)}), s32[2,64,1]{0,2,1:T(1,128)S(1)}, u32[]{:S(2)}, u32[]{:S(2)}) async-start(s32[2,64,1]{0,2,1:T(1,128)} %copy.84), calls=%async_computation | async-start | bytes 65536 | tf_op jit(solution)/shard_map/all_to_all | solution.py:82
  26.2 5.7 %copy-start.6 = (bf16[24,16,256]{2,1,0:T(8,128)(2,1)S(1)}, bf16[24,16,256]{2,1,0:T(8,128)(2,1)}, u32[]{:S(2)}) copy-start(bf16[24,16,256]{2,1,0:T(8,128)(2,1)} %param.20) | copy-start | bytes 589828
  26.2 5.7 %copy-start.7 = (bf16[24,16,256]{2,1,0:T(8,128)(2,1)S(1)}, bf16[24,16,256]{2,1,0:T(8,128)(2,1)}, u32[]{:S(2)}) copy-start(bf16[24,16,256]{2,1,0:T(8,128)(2,1)} %param.19) | copy-start | bytes 589828
  26.2 56.7 %all-to-all-start.2 = ((bf16[64,1,16,960]{3,2,1,0:T(8,128)(2,1)}), bf16[64,1,16,960]{3,2,1,0:T(8,128)(2,1)}, u32[]{:S(2)}, u32[]{:S(2)}) async-start(bf16[64,1,16,960]{3,2,1,0:T(8,128)(2,1)} %stack.2), calls=%async_computation.2 | async-start | bytes 4194304 | tf_op jit(solution)/shard_map/all_to_all | solution.py:80
  34.5 54.4 %copy-start.10 = (bf16[128,256]{1,0:T(8,128)(2,1)S(1)}, bf16[128,256]{1,0:T(8,128)(2,1)}, u32[]{:S(2)}) copy-start(bf16[128,256]{1,0:T(8,128)(2,1)} %param.18) | copy-start | bytes 196612
  34.5 55.1 %copy-start.13 = (s32[2,64]{1,0:T(2,128)S(1)}, s32[2,64]{1,0:T(2,128)}, u32[]{:S(2)}) copy-start(s32[2,64]{1,0:T(2,128)} %param.22) | copy-start | bytes 1540
  34.5 55.4 %copy-start.15 = (s32[1,2]{1,0:T(1,128)S(1)}, s32[1,2]{1,0:T(1,128)}, u32[]{:S(2)}) copy-start(s32[1,2]{1,0:T(1,128)} %param.23) | copy-start | bytes 28
  34.5 55.7 %copy-start.16 = (s32[64]{0:T(128)S(1)}, s32[64]{0:T(128)}, u32[]{:S(2)}) copy-start(s32[64]{0:T(128)} %param.25) | copy-start | bytes 772
  34.5 55.7 %copy-start.17 = (s32[1,2]{1,0:T(1,128)S(1)}, s32[1,2]{1,0:T(1,128)}, u32[]{:S(2)}) copy-start(s32[1,2]{1,0:T(1,128)} %param.24) | copy-start | bytes 28
  34.5 56.4 %copy-start.14 = (bf16[128,512]{1,0:T(8,128)(2,1)S(1)}, bf16[128,512]{1,0:T(8,128)(2,1)}, u32[]{:S(2)}) copy-start(bf16[128,512]{1,0:T(8,128)(2,1)} %param.16) | copy-start | bytes 393220
  82.9 57.0 %all-to-all-start.1 = ((bf16[2,64,16,512]{3,2,0,1:T(8,128)(2,1)}), bf16[2,64,16,512]{3,2,0,1:T(8,128)(2,1)S(1)}, u32[]{:S(2)}, u32[]{:S(2)}) async-start(bf16[2,64,16,512]{3,2,0,1:T(8,128)(2,1)} %copy.86), calls=%async_computation.1 | async-start | bytes 4194304 | tf_op jit(solution)/shard_map/all_to_all | solution.py:86
  95.6 44.6 %copy-start.5 = (bf16[2,16,960]{2,0,1:T(2,128)(2,1)}, bf16[2,16,960]{2,0,1:T(2,128)(2,1)S(1)}, u32[]{:S(2)}) copy-start(bf16[2,16,960]{2,0,1:T(2,128)(2,1)S(1)} %fusion.11) | copy-start | bytes 184324
  140.2 1.3 copy-start.1
  141.6 2.0 copy-start.2
  145.0 0.9 copy-start.8
  145.2 1.2 copy-start.4
  145.2 1.2 copy-start.11
  146.4 2.0 %copy-start.3 = (bf16[512,3584]{1,0:T(8,128)(2,1)S(1)}, bf16[512,3584]{1,0:T(8,128)(2,1)}, u32[]{:S(2)}) copy-start(bf16[512,3584]{1,0:T(8,128)(2,1)} %param.26) | copy-start | bytes 11010052
  148.4 1.3 slice-start
  151.2 35.1 %all-to-all-start.3 = ((bf16[8,128,512]{1,2,0:T(8,128)(2,1)}), bf16[8,128,512]{1,2,0:T(8,128)(2,1)S(1)}, u32[]{:S(2)}, u32[]{:S(2)}) async-start(bf16[8,128,512]{1,2,0:T(8,128)(2,1)} %maximum_maximum_fusion), calls=%async_computation.3 | async-start | bytes 2097152 | tf_op jit(solution)/shard_map/all_to_all | solution.py:135
  158.7 27.8 %slice-start.1 = ((bf16[2,16,960]{2,0,1:T(2,128)(2,1)}), bf16[2,16,448]{2,0,1:T(2,128)(2,1)S(1)}, s32[]{:S(2)}) async-start(bf16[2,16,960]{2,0,1:T(2,128)(2,1)} %copy-done.5), calls=%async_computation.5 | async-start | bytes 65536 | tf_op jit(solution)/shard_map/slice | solution.py:117
  186.4 16.1 %copy-start.9 = (bf16[128,448]{0,1:T(8,128)(2,1)S(1)}, bf16[128,448]{0,1:T(8,128)(2,1)}, u32[]{:S(2)}) copy-start(bf16[128,448]{0,1:T(8,128)(2,1)} %param.15) | copy-start | bytes 344068
  186.4 16.1 %copy-start.12 = (f32[448]{0:T(512)S(1)}, f32[448]{0:T(512)}, u32[]{:S(2)}) copy-start(f32[448]{0:T(512)} %param.29) | copy-start | bytes 5380
